TPU v7x, 128 devices: a whole 4x4x4 slice. The times are simulated.
128 devices in a mesh: row: 32 (over x_lo, z, y), col: 4 (over x_hi, core).
Axes of the slice: x: 4 (x_hi: 2, x_lo: 2; x = x_hi * 2 + x_lo), y: 4, z: 4, core: 2. Of those that a mesh axis runs over, the one named last changes fastest.
Arguments:
- inputs: bfloat16 [1024, 8192], P('row', 'col'), may hold values from -6 to 6
- out_grad: bfloat16 [1024, 8192], P('row', 'col'), may hold values from -4 to 4
- gate_pre: bfloat16 [1024, 28672], P('col', 'row'), may hold values from -6 to 6
- up_pre: bfloat16 [1024, 28672], P('col', 'row'), may hold values from -6 to 6
- gate_weight: bfloat16 [8192, 28672], P('col', 'row'), may hold values from -0.0625 to 0.0625
- up_weight: bfloat16 [8192, 28672], P('col', 'row'), may hold values from -0.0625 to 0.0625
- down_weight: bfloat16 [28672, 8192], P('row', 'col'), may hold values from -0.03125 to 0.03125
Outputs:
- grad_input: bfloat16 [1024, 8192], P('row', 'col')
- grad_gate: bfloat16 [8192, 28672], P('col', 'row')
- grad_up: bfloat16 [8192, 28672], P('col', 'row')
- grad_down: bfloat16 [28672, 8192], P('row', 'col')
All inputs are finite; a program needn't handle non-finite values.
Results may differ from a plain program's by a relative error of at most 0.005.
Values may be sent and summed in bfloat16 or wider, within the bound.
No kernel may reach another device: no remote copies, remote signals or barrier semaphores. Data moves between devices by JAX's collectives and lax.ppermute only.
A program may use at most 128 MiB of HBM per device.

v0:
```python
import jax
import jax.numpy as jnp
from jax import lax
from jax.sharding import PartitionSpec as P


def swiglu_back(hidden_grad, gate_stored, up_stored):
    gate_value = gate_stored.astype(jnp.float32)
    up_value = up_stored.astype(jnp.float32)
    sigmoid_gate = jax.nn.sigmoid(gate_value)
    activated = gate_value * sigmoid_gate
    hidden = (activated * up_value).astype(jnp.bfloat16)
    gate_grad = (
        hidden_grad * up_value * sigmoid_gate * (1.0 + gate_value * (1.0 - sigmoid_gate))
    ).astype(jnp.bfloat16)
    up_grad = (hidden_grad * activated).astype(jnp.bfloat16)
    return (hidden, gate_grad, up_grad)


def contract_last(left, right):
    return lax.dot_general(
        left, right, (((1,), (1,)), ((), ())), preferred_element_type=jnp.float32
    )


def contract_first(left, right):
    return lax.dot_general(
        left, right, (((0,), (0,)), ((), ())), preferred_element_type=jnp.float32
    )


def body(inputs, out_grad, gate_pre, up_pre, gate_weight, up_weight, down_weight):
    grad_rows = lax.all_gather(out_grad, "row", axis=0, tiled=True)
    partial_hidden = contract_last(grad_rows, down_weight)
    hidden_total = lax.psum(partial_hidden, "col")
    gate_all, up_all = (
        lax.all_gather(gate_pre, "col", axis=0, tiled=True),
        lax.all_gather(up_pre, "col", axis=0, tiled=True),
    )
    hidden, gate_grad, up_grad = swiglu_back(hidden_total, gate_all, up_all)
    grad_down = contract_first(hidden, grad_rows).astype(jnp.bfloat16)
    input_rows = lax.all_gather(inputs, "row", axis=0, tiled=True)
    gate_total = contract_first(input_rows, gate_grad)
    up_total = contract_first(input_rows, up_grad)
    input_total = lax.psum_scatter(
        contract_last(gate_grad, gate_weight) + contract_last(up_grad, up_weight),
        "row",
        scatter_dimension=0,
        tiled=True,
    )
    return (
        input_total.astype(jnp.bfloat16),
        gate_total.astype(jnp.bfloat16),
        up_total.astype(jnp.bfloat16),
        grad_down,
    )


def solution(mesh):
    in_specs = (
        P("row", "col"),
        P("row", "col"),
        P("col", "row"),
        P("col", "row"),
        P("col", "row"),
        P("col", "row"),
        P("row", "col"),
    )
    out_specs = (P("row", "col"), P("col", "row"), P("col", "row"), P("row", "col"))
    return jax.shard_map(body, mesh=mesh, in_specs=in_specs, out_specs=out_specs, check_vma=False)
```

profile of v0, /device:TPU:2, one launch (start us, length us, event | category | flops | bytes accessed | tf_op | source)
XLA Modules:
  0.0 658.2 jit_solution(382984773403680428)
XLA Ops:
  7.2 0.0 all-gather.5.cloned.1.call-start
  7.2 0.7 all-gather.5.cloned.1.call-update
  7.9 0.0 all-gather.9.cloned.1.call-start
  7.9 0.7 all-gather.9.cloned.1.call-update
  8.6 0.0 all-gather.7.cloned.1.call-start
  8.7 0.7 all-gather.7.cloned.1.call-update
  9.4 0.0 all-reduce.2.cloned.1.call-start
  9.4 158.3 %all-gather.5.cloned.1.call-done = bf16[1024,2048]{1,0:T(8,128)(2,1)} async-done(((bf16[32,2048]{1,0:T(8,128)(2,1)}), bf16[1024,2048]{1,0:T(8,128)(2,1)}) %all-gather.5.cloned.1.call-update) | async-done | bytes 4194320 | tf_op jit(solution)/shard_map/all_gather | solution.py:33
  167.8 9.7 %fusion.10 = f32[1024,896]{1,0:T(8,128)} fusion(bf16[1024,2048]{1,0:T(8,128)(2,1)} %all-gather.5.cloned.1.call-done, bf16[896,2048]{1,0:T(8,128)(2,1)} %param.13), kind=kOutput, calls=%fused_computation.19 | convolution fusion | flops 3758096384 | bytes 11534336 | tf_op jit(solution)/shard_map/dot_general | solution.py:21
  177.5 0.0 all-reduce.2.cloned.1.call-update
  177.5 0.0 all-gather.11.cloned.1.call-start
  177.5 0.5 all-gather.11.cloned.1.call-update
  178.1 0.0 reduce-scatter.2.cloned.1.call-start
  178.1 16.6 %all-gather.9.cloned.1.call-done = bf16[1024,896]{1,0:T(8,128)(2,1)} async-done(((bf16[256,896]{1,0:T(8,128)(2,1)}), bf16[1024,896]{1,0:T(8,128)(2,1)}) %all-gather.9.cloned.1.call-update) | async-done | bytes 1835024 | tf_op jit(solution)/shard_map/all_gather | solution.py:37
  194.7 26.3 %all-gather.7.cloned.1.call-done = bf16[1024,896]{1,0:T(8,128)(2,1)} async-done(((bf16[256,896]{1,0:T(8,128)(2,1)}), bf16[1024,896]{1,0:T(8,128)(2,1)}) %all-gather.7.cloned.1.call-update) | async-done | bytes 1835024 | tf_op jit(solution)/shard_map/all_gather | solution.py:38
  221.0 86.5 %all-reduce.2.cloned.1.call-done = f32[1024,896]{1,0:T(8,128)} async-done(((f32[1024,896]{1,0:T(8,128)}), f32[1024,896]{1,0:T(8,128)}) %all-reduce.2.cloned.1.call-update) | async-done | bytes 3670032 | tf_op jit(solution)/shard_map/psum | solution.py:35
  307.5 0.0 copy-start.3
  307.5 4.8 fusion.2
  312.3 0.0 copy-done.3
  312.3 0.0 copy-start.2
  312.4 0.0 copy-start
  312.4 0.0 copy-start.1
  312.4 0.0 copy-start.4
  312.4 6.9 %fusion.11 = f32[1024,2048]{1,0:T(8,128)} fusion(bf16[1024,896]{1,0:T(8,128)(2,1)S(1)} %fusion.2, bf16[2048,896]{1,0:T(8,128)(2,1)S(1)} %copy-done.3), kind=kOutput, calls=%fused_computation.20 | convolution fusion | flops 3758096384 | bytes 13893632 | tf_op jit(solution)/shard_map/dot_general | solution.py:21
  319.3 0.0 copy-done.2
  319.3 0.0 copy-done
  319.3 0.0 copy-done.1
  319.3 0.0 copy-done.4
  319.3 9.2 %convolution_add_fusion = f32[1024,2048]{1,0:T(8,128)} fusion(f32[1024,2048]{1,0:T(8,128)} %fusion.11, bf16[2048,896]{1,0:T(8,128)(2,1)S(1)} %copy-done.4, f32[1024,896]{1,0:T(8,128)S(1)} %copy-done, bf16[1024,896]{1,0:T(8,128)(2,1)S(1)} %copy-done.1), kind=kOutput, calls=%fused_computation.5 | convolution fusion | flops 3766616064 | bytes 25952256 | tf_op jit(solution)/shard_map/dot_general | solution.py:21
  328.5 0.0 reduce-scatter.2.cloned.1.call-update
  328.5 8.8 %convolution_convert_fusion = bf16[896,2048]{1,0:T(8,128)(2,1)} fusion(bf16[1024,2048]{1,0:T(8,128)(2,1)} %all-gather.5.cloned.1.call-done, bf16[1024,896]{1,0:T(8,128)(2,1)} %all-gather.7.cloned.1.call-done, bf16[1024,896]{1,0:T(8,128)(2,1)S(1)} %copy-done.1), kind=kOutput, calls=%fused_computation.17 | convolution fusion | flops 3767271424 | bytes 11534336 | tf_op jit(solution)/shard_map/dot_general | solution.py:27
  337.3 127.8 %all-gather.11.cloned.1.call-done = bf16[1024,2048]{1,0:T(8,128)(2,1)} async-done(((bf16[32,2048]{1,0:T(8,128)(2,1)}), bf16[1024,2048]{1,0:T(8,128)(2,1)}) %all-gather.11.cloned.1.call-update) | async-done | bytes 4194320 | tf_op jit(solution)/shard_map/all_gather | solution.py:42
  465.2 8.6 %convert_bitcast_fusion.1 = bf16[2048,896]{0,1:T(8,128)(2,1)} fusion(bf16[1024,896]{1,0:T(8,128)(2,1)} %copy-done.2, bf16[1024,2048]{1,0:T(8,128)(2,1)} %all-gather.11.cloned.1.call-done), kind=kOutput, calls=%fused_computation.15 | convolution fusion | flops 3759931392 | bytes 9699328 | tf_op jit(solution)/shard_map/dot_general | solution.py:27
  473.8 6.1 copy.11
  479.9 9.3 %convert_bitcast_fusion = bf16[2048,896]{0,1:T(8,128)(2,1)} fusion(bf16[1024,2048]{1,0:T(8,128)(2,1)} %all-gather.11.cloned.1.call-done, f32[1024,896]{1,0:T(8,128)} %all-reduce.2.cloned.1.call-done, bf16[1024,896]{1,0:T(8,128)(2,1)S(1)} %copy-done.1), kind=kOutput, calls=%fused_computation.14 | convolution fusion | flops 3766353920 | bytes 13369344 | tf_op jit(solution)/shard_map/dot_general | solution.py:27
  489.1 6.1 copy.12
  495.2 154.5 %reduce-scatter.2.cloned.1.call-done = f32[32,2048]{1,0:T(8,128)} async-done(((f32[1024,2048]{1,0:T(8,128)}), f32[32,2048]{1,0:T(8,128)}) %reduce-scatter.2.cloned.1.call-update) | async-done | bytes 262160 | tf_op jit(solution)/shard_map/reduce_scatter | solution.py:45
  649.7 1.6 convert_element_type.37
Async XLA Ops:
  7.2 160.6 %all-gather.5.cloned.1.call-start = ((), (), s32[]{:S(2)}) async-start(), calls=%async_computation.1 | async-start | bytes 4325376 | tf_op jit(solution)/shard_map/all_gather | solution.py:33
  7.9 186.8 %all-gather.9.cloned.1.call-start = ((), (), s32[]{:S(2)}) async-start(), calls=%async_computation.4 | async-start | bytes 2293760 | tf_op jit(solution)/shard_map/all_gather | solution.py:37
  8.6 212.3 %all-gather.7.cloned.1.call-start = ((), (), s32[]{:S(2)}) async-start(), calls=%async_computation.3 | async-start | bytes 2293760 | tf_op jit(solution)/shard_map/all_gather | solution.py:38
  9.4 298.1 %all-reduce.2.cloned.1.call-start = ((), (), s32[]{:S(2)}) async-start(), calls=%async_computation.2 | async-start | bytes 7340032 | tf_op jit(solution)/shard_map/psum | solution.py:35
  177.5 287.7 %all-gather.11.cloned.1.call-start = ((), (), s32[]{:S(2)}) async-start(), calls=%async_computation.6 | async-start | bytes 4325376 | tf_op jit(solution)/shard_map/all_gather | solution.py:42
  178.1 471.6 %reduce-scatter.2.cloned.1.call-start = ((), (), s32[]{:S(2)}) async-start(), calls=%async_computation.5 | async-start | bytes 8650752 | tf_op jit(solution)/shard_map/reduce_scatter | solution.py:45
  307.5 4.8 copy-start.3
  312.3 7.0 %copy-start.2 = (bf16[1024,896]{1,0:T(8,128)(2,1)}, bf16[1024,896]{1,0:T(8,128)(2,1)S(1)}, u32[]{:S(2)}) copy-start(bf16[1024,896]{1,0:T(8,128)(2,1)S(1)} %fusion.2) | copy-start | bytes 5505028
  312.4 7.0 %copy-start = (f32[1024,896]{1,0:T(8,128)S(1)}, f32[1024,896]{1,0:T(8,128)}, u32[]{:S(2)}) copy-start(f32[1024,896]{1,0:T(8,128)} %all-reduce.2.cloned.1.call-done) | copy-start | bytes 11010052
  312.4 6.9 %copy-start.1 = (bf16[1024,896]{1,0:T(8,128)(2,1)S(1)}, bf16[1024,896]{1,0:T(8,128)(2,1)}, u32[]{:S(2)}) copy-start(bf16[1024,896]{1,0:T(8,128)(2,1)} %all-gather.9.cloned.1.call-done) | copy-start | bytes 5505028
  312.4 6.9 %copy-start.4 = (bf16[2048,896]{1,0:T(8,128)(2,1)S(1)}, bf16[2048,896]{1,0:T(8,128)(2,1)}, u32[]{:S(2)}) copy-start(bf16[2048,896]{1,0:T(8,128)(2,1)} %param.12) | copy-start | bytes 11010052
Sparse Core Ops, SparseCore 0:
  9.6 158.1 all-gather.4
  169.4 25.2 all-gather.8
  196.4 24.5 all-gather.6
  223.9 83.5 all-reduce.1
  309.0 156.1 all-gather.10
  467.4 182.2 reduce-scatter.1
where the time goes:
time: 659 us; the launch traced here: 658 us
  waiting for transfers between devices  573 us (87%)
  matrix products  52.5 us (8%)
  between operations  14.2 us (2%)
  local copies, waits for them, and re-layouts  12.2 us (2%)
    all_gather x1, waiting for transfers between devices, body(): grad_rows = lax.all_gather(out_grad, 'row', axis=0, tiled=True)  158 us
    reduce_scatter x1, waiting for transfers between devices, body(): lax.psum_scatter(contract_last(gate_grad, gate_weight) + contract_last(up...  155 us
    all_gather x1, waiting for transfers between devices, body(): input_rows = lax.all_gather(inputs, 'row', axis=0, tiled=True)  128 us
    psum x1, waiting for transfers between devices, body(): hidden_total = lax.psum(partial_hidden, 'col')  86.5 us
    dot_general x3, matrix products, contract_first(): lax.dot_general(left, right, (((0,), (0,)), ((), ())), preferred_element_...  26.7 us
    all_gather x1, waiting for transfers between devices, body(): lax.all_gather(up_pre, 'col', axis=0, tiled=True)  26.3 us
    dot_general x3, matrix products, contract_last(): lax.dot_general(left, right, (((1,), (1,)), ((), ())), preferred_element_...  25.7 us
    all_gather x1, waiting for transfers between devices, body(): lax.all_gather(gate_pre, 'col', axis=0, tiled=True)  16.6 us
  transfers between devices with their start and end apart: 6, of which 6 were waited for; matrix products, arithmetic and copies ran while one was open for 11% of the time, Pallas kernels for 0%

commit v1 on v0

v1 whole, which is shorter than its diff:
```python
import jax
import jax.numpy as jnp
from jax import lax
from jax.sharding import PartitionSpec as P


def swiglu_back(hidden_grad, gate_stored, up_stored):
    gate_value = gate_stored.astype(jnp.float32)
    up_value = up_stored.astype(jnp.float32)
    sigmoid_gate = jax.nn.sigmoid(gate_value)
    activated = gate_value * sigmoid_gate
    hidden = (activated * up_value).astype(jnp.bfloat16)
    gate_grad = (
        hidden_grad * up_value * sigmoid_gate * (1.0 + gate_value * (1.0 - sigmoid_gate))
    ).astype(jnp.bfloat16)
    up_grad = (hidden_grad * activated).astype(jnp.bfloat16)
    return (hidden, gate_grad, up_grad)


def contract_last(left, right):
    return lax.dot_general(
        left, right, (((1,), (1,)), ((), ())), preferred_element_type=jnp.float32
    )


def contract_first(left, right):
    return lax.dot_general(
        left, right, (((0,), (0,)), ((), ())), preferred_element_type=jnp.float32
    )


def gather_rows(block, axis, count):
    tiled = jnp.tile(block, (count, 1))
    return lax.all_to_all(tiled, axis, 0, 0, tiled=True)


def scatter_sum_rows(partial, axis, count):
    received = lax.all_to_all(partial, axis, 0, 0, tiled=True)
    return received.reshape((count, partial.shape[0] // count) + partial.shape[1:]).sum(0)


def make_body(rows):
    def body(inputs, out_grad, gate_pre, up_pre, gate_weight, up_weight, down_weight):
        grad_rows = gather_rows(out_grad, "row", rows)
        width = gate_pre.shape[1]
        pre_all = lax.all_gather(
            jnp.concatenate([gate_pre, up_pre], axis=1), "col", axis=0, tiled=True
        )
        gate_all, up_all = pre_all[:, :width], pre_all[:, width:]
        partial_hidden = contract_last(grad_rows, down_weight)
        hidden_total = lax.psum(partial_hidden, "col")
        hidden, gate_grad, up_grad = swiglu_back(hidden_total, gate_all, up_all)
        grad_down = contract_first(hidden, grad_rows).astype(jnp.bfloat16)
        input_rows = gather_rows(inputs, "row", rows)
        gate_total = contract_first(input_rows, gate_grad)
        up_total = contract_first(input_rows, up_grad)
        input_total = scatter_sum_rows(
            contract_last(gate_grad, gate_weight) + contract_last(up_grad, up_weight),
            "row",
            rows,
        )
        return (
            input_total.astype(jnp.bfloat16),
            gate_total.astype(jnp.bfloat16),
            up_total.astype(jnp.bfloat16),
            grad_down,
        )

    return body


def solution(mesh):
    in_specs = (
        P("row", "col"),
        P("row", "col"),
        P("col", "row"),
        P("col", "row"),
        P("col", "row"),
        P("col", "row"),
        P("row", "col"),
    )
    out_specs = (P("row", "col"), P("col", "row"), P("col", "row"), P("row", "col"))
    body = make_body(mesh.shape["row"])
    return jax.shard_map(body, mesh=mesh, in_specs=in_specs, out_specs=out_specs, check_vma=False)
```

time: 659 us -> 387 us (0.59)
  waiting for transfers between devices: 573 us -> 200 us
  blocking collectives: 0 us -> 78.1 us
  starting transfers between devices: 0.23 us -> 15.7 us
  local copies, waits for them, and re-layouts: 12.2 us -> 19 us
    all_gather x4 -> x1, waiting for transfers between devices: 329 us -> 0.02 us  [body(): lax.all_gather(jnp.concatenate([gate_pre, up_pre], axis=1), 'col', axis=0...]
    reduce_scatter x1 -> x0, waiting for transfers between devices: 155 us -> none  [body(): lax.psum_scatter(contract_last(gate_grad, gate_weight) + contract_last(up...]
    all_to_all x0 -> x2, waiting for transfers between devices: none -> 95.5 us  [the longest x1 95.5 us: scatter_sum_rows(): received = lax.all_to_all(partial, axis, 0, 0, tiled=True)]
    all_to_all x0 -> x1, blocking collectives: none -> 78.1 us  [gather_rows(): return lax.all_to_all(tiled, axis, 0, 0, tiled=True)]
    psum x1, waiting for transfers between devices: 86.5 us -> 105 us  [body(): hidden_total = lax.psum(partial_hidden, 'col')]
    all_to_all x0 -> x2, starting transfers between devices: none -> 15.7 us  [the longest x1 9.59 us: scatter_sum_rows(): received = lax.all_to_all(partial, axis, 0, 0, tiled=True)]
    unnamed x12 -> x20, local copies, waits for them, and re-layouts: 12.2 us -> 15.1 us
  transfers between devices with their start and end apart: 6 -> 4, of which waited for: 6 -> 2; matrix products, arithmetic and copies ran while one was open for 11% -> 18% of each run, Pallas kernels for 0% -> 0%
where the time goes in v1:
time: 387 us; the launch traced here: 386 us
  waiting for transfers between devices  200 us (52%)
  blocking collectives  78.1 us (20%)
  matrix products  47.9 us (12%)
  local copies, waits for them, and re-layouts  19 us (5%)
  starting transfers between devices  15.7 us (4%)
  between operations  14.1 us (4%)
  other arithmetic  10.7 us (3%)
    psum x1, waiting for transfers between devices, body(): hidden_total = lax.psum(partial_hidden, 'col')  105 us
    all_to_all x1, waiting for transfers between devices, scatter_sum_rows(): received = lax.all_to_all(partial, axis, 0, 0, tiled=True)  95.5 us
    all_to_all x1, blocking collectives, gather_rows(): return lax.all_to_all(tiled, axis, 0, 0, tiled=True)  78.1 us
    dot_general x3, matrix products, contract_first(): lax.dot_general(left, right, (((0,), (0,)), ((), ())), preferred_element_...  25.8 us
    dot_general x3, matrix products, contract_last(): lax.dot_general(left, right, (((1,), (1,)), ((), ())), preferred_element_...  22.1 us
    unnamed x20, local copies, waits for them, and re-layouts  15.1 us
    all_to_all x1, starting transfers between devices, scatter_sum_rows(): received = lax.all_to_all(partial, axis, 0, 0, tiled=True)  9.59 us
  transfers between devices with their start and end apart: 4, of which 2 were waited for; matrix products, arithmetic and copies ran while one was open for 18% of the time, Pallas kernels for 0%

profile of v1, /device:TPU:2, one launch (start us, length us, event | category | flops | bytes accessed | tf_op | source)
XLA Modules:
  0.0 385.9 jit_solution(6980774877278166262)
XLA Ops:
  7.2 0.0 all-gather.2.cloned.1.call-start
  7.2 2.2 pad_maximum_fusion
  9.4 0.0 all-gather.2.cloned.1.call-update
  9.4 0.0 all-reduce.2.cloned.1.call-start
  9.4 1.4 tile.4
  10.9 0.0 copy-start.6
  10.9 78.1 %all_to_all.27 = bf16[32,32,2048]{2,1,0:T(8,128)(2,1)S(1)} all-to-all(bf16[32,32,2048]{2,1,0:T(8,128)(2,1)S(1)} %tile.4), channel_id=1, replica_groups=mesh['row'=32,'col'=4] {'row'}, dimensions={0} | all-to-all | bytes 8388608 | tf_op jit(solution)/shard_map/all_to_all | solution.py:34
  89.0 0.0 copy-start
  89.0 2.0 copy-done
  91.0 0.0 copy-done.6
  91.0 6.4 %fusion.11 = f32[1024,896]{1,0:T(8,128)} fusion(bf16[1024,2048]{1,0:T(8,128)(2,1)S(1)} %bitcast.17, bf16[896,2048]{1,0:T(8,128)(2,1)S(1)} %copy-done.6), kind=kOutput, calls=%fused_computation.21 | convolution fusion | flops 3758096384 | bytes 11534336 | tf_op jit(solution)/shard_map/dot_general | solution.py:21
  97.3 0.0 copy-start.5
  97.3 0.0 all-reduce.2.cloned.1.call-update
  97.4 0.9 copy-done.5
  98.3 2.5 tile.5
  100.7 6.1 %all-to-all-start.2 = ((bf16[32,32,2048]{2,1,0:T(8,128)(2,1)}), bf16[32,32,2048]{2,1,0:T(8,128)(2,1)}, u32[]{:S(2)}, u32[]{:S(2)}) async-start(bf16[32,32,2048]{2,1,0:T(8,128)(2,1)} %tile.5), calls=%async_computation.2 | async-start | bytes 8388608 | tf_op jit(solution)/shard_map/all_to_all | solution.py:34
  106.8 0.0 all-gather.2.cloned.1.call-done
  106.8 104.8 %all-reduce.2.cloned.1.call-done = f32[1024,896]{1,0:T(8,128)} async-done(((f32[1024,896]{1,0:T(8,128)}), f32[1024,896]{1,0:T(8,128)}) %all-reduce.2.cloned.1.call-update) | async-done | bytes 3670032 | tf_op jit(solution)/shard_map/psum | solution.py:51
  211.6 0.0 copy-start.7
  211.6 4.0 %fusion.2 = bf16[1024,896]{1,0:T(8,128)(2,1)S(1)} fusion(f32[1024,896]{1,0:T(8,128)} %all-reduce.2.cloned.1.call-done, bf16[1024,1792]{1,0:T(8,128)(2,1)} %all-gather.2.cloned.1.call-done), kind=kLoop, calls=%fused_computation.8 | loop fusion | flops 11010048 | bytes 9175040 | tf_op jit(solution)/shard_map/convert_element_type | solution.py:15
  215.6 0.2 copy-done.7
  215.8 0.0 copy-start.1
  215.8 0.0 copy-start.3
  215.8 0.0 copy-start.8
  215.8 6.7 %fusion.12 = f32[1024,2048]{1,0:T(8,128)} fusion(bf16[1024,896]{1,0:T(8,128)(2,1)S(1)} %fusion.2, bf16[2048,896]{1,0:T(8,128)(2,1)S(1)} %copy-done.7), kind=kOutput, calls=%fused_computation.22 | convolution fusion | flops 3758096384 | bytes 13893632 | tf_op jit(solution)/shard_map/dot_general | solution.py:21
  222.5 0.0 copy-done.1
  222.5 0.0 copy-done.3
  222.5 0.0 copy-done.8
  222.5 9.0 %convolution_add_fusion = f32[1024,2048]{1,0:T(8,128)} fusion(f32[1024,2048]{1,0:T(8,128)} %fusion.12, bf16[2048,896]{1,0:T(8,128)(2,1)S(1)} %copy-done.8, f32[1024,896]{1,0:T(8,128)S(1)} %copy-done.3, bf16[1024,1792]{1,0:T(8,128)(2,1)S(1)} %copy-done.1), kind=kOutput, calls=%fused_computation.5 | convolution fusion | flops 3766616064 | bytes 25952256 | tf_op jit(solution)/shard_map/dot_general | solution.py:21
  231.5 0.0 all-to-all-done.2
  231.5 9.6 %all-to-all-start.1 = ((f32[32,32,2048]{2,1,0:T(8,128)}), f32[32,32,2048]{2,1,0:T(8,128)}, u32[]{:S(2)}, u32[]{:S(2)}) async-start(f32[32,32,2048]{2,1,0:T(8,128)} %bitcast.16), calls=%async_computation.1 | async-start | bytes 16777216 | tf_op jit(solution)/shard_map/all_to_all | solution.py:38
  241.1 0.0 copy-start.2
  241.1 0.0 copy-start.4
  241.1 9.5 %convolution_convert_fusion = bf16[896,2048]{1,0:T(8,128)(2,1)} fusion(bf16[1024,2048]{1,0:T(8,128)(2,1)} %bitcast.18, bf16[1024,1792]{1,0:T(8,128)(2,1)} %all-gather.2.cloned.1.call-done), kind=kOutput, calls=%fused_computation.17 | convolution fusion | flops 3767271424 | bytes 11534336 | tf_op jit(solution)/shard_map/dot_general | solution.py:27
  250.7 0.0 copy-done.2
  250.7 0.0 copy-done.4
  250.7 8.3 %convert_bitcast_fusion = bf16[2048,896]{0,1:T(8,128)(2,1)} fusion(bf16[1024,2048]{1,0:T(8,128)(2,1)} %bitcast.2, f32[1024,896]{1,0:T(8,128)S(1)} %copy-done.4, bf16[1024,1792]{1,0:T(8,128)(2,1)S(1)} %copy-done.2), kind=kOutput, calls=%fused_computation.14 | convolution fusion | flops 3766353920 | bytes 13369344 | tf_op jit(solution)/shard_map/dot_general | solution.py:27
  259.0 6.0 %copy.12 = bf16[2048,896]{1,0:T(8,128)(2,1)} copy(bf16[2048,896]{0,1:T(8,128)(2,1)} %convert_bitcast_fusion) | data formatting | bytes 7340032
  265.0 8.0 %convert_bitcast_fusion.1 = bf16[2048,896]{0,1:T(8,128)(2,1)} fusion(bf16[1024,896]{1,0:T(8,128)(2,1)S(1)} %fusion.2, bf16[1024,2048]{1,0:T(8,128)(2,1)} %bitcast.2), kind=kOutput, calls=%fused_computation.15 | convolution fusion | flops 3759931392 | bytes 9699328 | tf_op jit(solution)/shard_map/dot_general | solution.py:27
  273.0 6.0 %copy.11 = bf16[2048,896]{1,0:T(8,128)(2,1)} copy(bf16[2048,896]{0,1:T(8,128)(2,1)} %convert_bitcast_fusion.1) | data formatting | bytes 7340032
  279.0 95.5 %all-to-all-done.1 = f32[32,32,2048]{2,1,0:T(8,128)} async-done(((f32[32,32,2048]{2,1,0:T(8,128)}), f32[32,32,2048]{2,1,0:T(8,128)}, u32[]{:S(2)}, u32[]{:S(2)}) %all-to-all-start.1) | async-done | bytes 8388640 | tf_op jit(solution)/shard_map/all_to_all | solution.py:38
  374.5 4.5 %reduce_sum.9 = bf16[32,2048]{1,0:T(8,128)(2,1)} reduce(f32[32,32,2048]{2,1,0:T(8,128)} %all-to-all-done.1, f32[]{:T(128)} %constant.1.clone.1), dimensions={0}, to_apply=%region_1.0 | reduce | flops 2031616 | bytes 8519684 | tf_op jit(solution)/shard_map/reduce_sum | solution.py:39
Async XLA Ops:
  7.2 99.7 %all-gather.2.cloned.1.call-start = ((), (), s32[]{:S(2)}) async-start(), calls=%async_computation.4 | async-start | bytes 4587520 | tf_op jit(solution)/shard_map/all_gather | solution.py:46
  9.4 202.2 %all-reduce.2.cloned.1.call-start = ((), (), s32[]{:S(2)}) async-start(), calls=%async_computation.3 | async-start | bytes 7340032 | tf_op jit(solution)/shard_map/psum | solution.py:51
  10.9 80.1 %copy-start.6 = (bf16[896,2048]{1,0:T(8,128)(2,1)S(1)}, bf16[896,2048]{1,0:T(8,128)(2,1)}, u32[]{:S(2)}) copy-start(bf16[896,2048]{1,0:T(8,128)(2,1)} %param.13) | copy-start | bytes 11010052
  89.0 2.0 copy-start
  97.3 0.9 copy-start.5
  100.7 130.8 %all-to-all-start.2 = ((bf16[32,32,2048]{2,1,0:T(8,128)(2,1)}), bf16[32,32,2048]{2,1,0:T(8,128)(2,1)}, u32[]{:S(2)}, u32[]{:S(2)}) async-start(bf16[32,32,2048]{2,1,0:T(8,128)(2,1)} %tile.5), calls=%async_computation.2 | async-start | bytes 8388608 | tf_op jit(solution)/shard_map/all_to_all | solution.py:34
  211.6 4.2 %copy-start.7 = (bf16[2048,896]{1,0:T(8,128)(2,1)S(1)}, bf16[2048,896]{1,0:T(8,128)(2,1)}, u32[]{:S(2)}) copy-start(bf16[2048,896]{1,0:T(8,128)(2,1)} %param.11) | copy-start | bytes 11010052
  215.8 6.7 %copy-start.1 = (bf16[1024,1792]{1,0:T(8,128)(2,1)S(1)}, bf16[1024,1792]{1,0:T(8,128)(2,1)}, u32[]{:S(2)}) copy-start(bf16[1024,1792]{1,0:T(8,128)(2,1)} %all-gather.2.cloned.1.call-done) | copy-start | bytes 11010052
  215.8 6.7 %copy-start.3 = (f32[1024,896]{1,0:T(8,128)S(1)}, f32[1024,896]{1,0:T(8,128)}, u32[]{:S(2)}) copy-start(f32[1024,896]{1,0:T(8,128)} %all-reduce.2.cloned.1.call-done) | copy-start | bytes 11010052
  215.8 6.7 %copy-start.8 = (bf16[2048,896]{1,0:T(8,128)(2,1)S(1)}, bf16[2048,896]{1,0:T(8,128)(2,1)}, u32[]{:S(2)}) copy-start(bf16[2048,896]{1,0:T(8,128)(2,1)} %param.12) | copy-start | bytes 11010052
  231.5 143.0 %all-to-all-start.1 = ((f32[32,32,2048]{2,1,0:T(8,128)}), f32[32,32,2048]{2,1,0:T(8,128)}, u32[]{:S(2)}, u32[]{:S(2)}) async-start(f32[32,32,2048]{2,1,0:T(8,128)} %bitcast.16), calls=%async_computation.1 | async-start | bytes 16777216 | tf_op jit(solution)/shard_map/all_to_all | solution.py:38
  241.1 9.6 %copy-start.2 = (bf16[1024,1792]{1,0:T(8,128)(2,1)S(1)}, bf16[1024,1792]{1,0:T(8,128)(2,1)}, u32[]{:S(2)}) copy-start(bf16[1024,1792]{1,0:T(8,128)(2,1)} %all-gather.2.cloned.1.call-done) | copy-start | bytes 11010052
  241.1 9.5 %copy-start.4 = (f32[1024,896]{1,0:T(8,128)S(1)}, f32[1024,896]{1,0:T(8,128)}, u32[]{:S(2)}) copy-start(f32[1024,896]{1,0:T(8,128)} %all-reduce.2.cloned.1.call-done) | copy-start | bytes 11010052
Sparse Core Ops, SparseCore 0:
  10.2 56.7 all-gather.1
  97.5 114.0 all-reduce.1

commit v2 on v1

--- a/solution.py
+++ b/solution.py
@@ -35,11 +35,17 @@
 
 
 def scatter_sum_rows(partial, axis, count):
-    received = lax.all_to_all(partial, axis, 0, 0, tiled=True)
-    return received.reshape((count, partial.shape[0] // count) + partial.shape[1:]).sum(0)
+    received = lax.all_to_all(partial.astype(jnp.bfloat16), axis, 0, 0, tiled=True)
+    received = received.reshape((count, partial.shape[0] // count) + partial.shape[1:])
+    return received.astype(jnp.float32).sum(0)
 
 
-def make_body(rows):
+def sum_all(partial, axis, count):
+    total = scatter_sum_rows(partial, axis, count)
+    return gather_rows(total.astype(jnp.bfloat16), axis, count).astype(jnp.float32)
+
+
+def make_body(rows, cols):
     def body(inputs, out_grad, gate_pre, up_pre, gate_weight, up_weight, down_weight):
         grad_rows = gather_rows(out_grad, "row", rows)
         width = gate_pre.shape[1]
@@ -48,7 +54,7 @@
         )
         gate_all, up_all = pre_all[:, :width], pre_all[:, width:]
         partial_hidden = contract_last(grad_rows, down_weight)
-        hidden_total = lax.psum(partial_hidden, "col")
+        hidden_total = sum_all(partial_hidden, "col", cols)
         hidden, gate_grad, up_grad = swiglu_back(hidden_total, gate_all, up_all)
         grad_down = contract_first(hidden, grad_rows).astype(jnp.bfloat16)
         input_rows = gather_rows(inputs, "row", rows)
@@ -80,5 +86,5 @@
         P("row", "col"),
     )
     out_specs = (P("row", "col"), P("col", "row"), P("col", "row"), P("row", "col"))
-    body = make_body(mesh.shape["row"])
+    body = make_body(mesh.shape["row"], mesh.shape["col"])
     return jax.shard_map(body, mesh=mesh, in_specs=in_specs, out_specs=out_specs, check_vma=False)

time: 387 us -> 293 us (0.76)
  waiting for transfers between devices: 200 us -> 126 us
  blocking collectives: 78.1 us -> 54.4 us
  starting transfers between devices: 15.7 us -> 25.2 us
    all_to_all x1 -> x2, waiting for transfers between devices: 0.01 us -> 107 us  [gather_rows(): return lax.all_to_all(tiled, axis, 0, 0, tiled=True)]
    psum x1 -> x0, waiting for transfers between devices: 105 us -> none  [body(): hidden_total = lax.psum(partial_hidden, 'col')]
    all_to_all x1, waiting for transfers between devices: 95.5 us -> 18.5 us  [scatter_sum_rows(): lax.all_to_all(partial.astype(jnp.bfloat16), axis, 0, 0, tiled=True)]
    all_to_all x1, blocking collectives: 78.1 us -> 26.8 us  [gather_rows(): return lax.all_to_all(tiled, axis, 0, 0, tiled=True)]
    all_to_all x0 -> x1, blocking collectives: none -> 27.6 us  [scatter_sum_rows(): lax.all_to_all(partial.astype(jnp.bfloat16), axis, 0, 0, tiled=True)]
    all_to_all x1 -> x2, starting transfers between devices: 6.08 us -> 19.4 us  [gather_rows(): return lax.all_to_all(tiled, axis, 0, 0, tiled=True)]
  transfers between devices with their start and end apart: 4 -> 4, of which waited for: 2 -> 3; matrix products, arithmetic and copies ran while one was open for 18% -> 22% of each run, Pallas kernels for 0% -> 0%
where the time goes in v2:
time: 293 us; the launch traced here: 291 us
  waiting for transfers between devices  126 us (43%)
  blocking collectives  54.4 us (19%)
  matrix products  44.1 us (15%)
  starting transfers between devices  25.2 us (9%)
  local copies, waits for them, and re-layouts  18.3 us (6%)
  between operations  14.2 us (5%)
  other arithmetic  8.83 us (3%)
    all_to_all x2, waiting for transfers between devices, gather_rows(): return lax.all_to_all(tiled, axis, 0, 0, tiled=True)  107 us
    all_to_all x1, blocking collectives, scatter_sum_rows(): lax.all_to_all(partial.astype(jnp.bfloat16), axis, 0, 0, tiled=True)  27.6 us
    all_to_all x1, blocking collectives, gather_rows(): return lax.all_to_all(tiled, axis, 0, 0, tiled=True)  26.8 us
    dot_general x3, matrix products, contract_first(): lax.dot_general(left, right, (((0,), (0,)), ((), ())), preferred_element_...  25.6 us
    all_to_all x2, starting transfers between devices, gather_rows(): return lax.all_to_all(tiled, axis, 0, 0, tiled=True)  19.4 us
    dot_general x3, matrix products, contract_last(): lax.dot_general(left, right, (((1,), (1,)), ((), ())), preferred_element_...  18.5 us
    all_to_all x1, waiting for transfers between devices, scatter_sum_rows(): lax.all_to_all(partial.astype(jnp.bfloat16), axis, 0, 0, tiled=True)  18.5 us
    unnamed x20, local copies, waits for them, and re-layouts  12.3 us
  transfers between devices with their start and end apart: 4, of which 3 were waited for; matrix products, arithmetic and copies ran while one was open for 22% of the time, Pallas kernels for 0%

profile of v2, /device:TPU:2, one launch (start us, length us, event | category | flops | bytes accessed | tf_op | source)
XLA Modules:
  0.0 290.6 jit_solution(1323969768076005935)
XLA Ops:
  7.2 3.4 %tile.6 = bf16[32,32,2048]{2,1,0:T(8,128)(2,1)} broadcast(bf16[32,2048]{1,0:T(8,128)(2,1)} %param.8), dimensions={1,2} | broadcast | bytes 4325376 | tf_op jit(solution)/shard_map/tile | solution.py:33
  10.6 0.0 copy-start.4
  10.6 0.0 copy-start.5
  10.6 9.8 %all-to-all-start = ((bf16[32,32,2048]{2,1,0:T(8,128)(2,1)}), bf16[32,32,2048]{2,1,0:T(8,128)(2,1)}, u32[]{:S(2)}, u32[]{:S(2)}) async-start(bf16[32,32,2048]{2,1,0:T(8,128)(2,1)} %tile.6), calls=%async_computation | async-start | bytes 8388608 | tf_op jit(solution)/shard_map/all_to_all | solution.py:34
  20.3 0.0 all-gather.2.cloned.1.call-start
  20.4 0.0 copy-done.4
  20.4 0.0 copy-done.5
  20.4 1.0 pad_maximum_fusion
  21.4 0.0 all-gather.2.cloned.1.call-update
  21.4 66.4 %all-to-all-done = bf16[32,32,2048]{2,1,0:T(8,128)(2,1)} async-done(((bf16[32,32,2048]{2,1,0:T(8,128)(2,1)}), bf16[32,32,2048]{2,1,0:T(8,128)(2,1)}, u32[]{:S(2)}, u32[]{:S(2)}) %all-to-all-start) | async-done | bytes 4194336 | tf_op jit(solution)/shard_map/all_to_all | solution.py:34
  87.8 7.8 %convolution_convert_fusion.1 = bf16[1024,896]{1,0:T(8,128)(2,1)S(1)} fusion(bf16[1024,2048]{1,0:T(8,128)(2,1)} %bitcast, bf16[896,2048]{1,0:T(8,128)(2,1)} %param.13), kind=kOutput, calls=%fused_computation.19 | convolution fusion | flops 3759013888 | bytes 9699328 | tf_op jit(solution)/shard_map/dot_general | solution.py:21
  95.6 27.6 %all_to_all.42 = bf16[4,256,896]{2,1,0:T(8,128)(2,1)S(1)} all-to-all(bf16[4,256,896]{2,1,0:T(8,128)(2,1)S(1)} %bitcast.24), channel_id=1, replica_groups=mesh['row'=32,'col'=4] {'col'}, dimensions={0} | all-to-all | bytes 3670016 | tf_op jit(solution)/shard_map/all_to_all | solution.py:38
  123.2 0.0 copy-start.6
  123.2 0.5 reduce_sum.24
  123.7 0.1 tile.7
  123.9 26.8 %all_to_all.43 = bf16[4,256,896]{2,1,0:T(8,128)(2,1)S(1)} all-to-all(bf16[4,256,896]{2,1,0:T(8,128)(2,1)S(1)} %tile.7), channel_id=1, replica_groups=mesh['row'=32,'col'=4] {'col'}, dimensions={0} | all-to-all | bytes 3670016 | tf_op jit(solution)/shard_map/all_to_all | solution.py:34
  150.7 0.0 copy-done.6
  150.7 2.5 tile.8
  153.1 9.6 %all-to-all-start.4 = ((bf16[32,32,2048]{2,1,0:T(8,128)(2,1)}), bf16[32,32,2048]{2,1,0:T(8,128)(2,1)}, u32[]{:S(2)}, u32[]{:S(2)}) async-start(bf16[32,32,2048]{2,1,0:T(8,128)(2,1)} %tile.8), calls=%async_computation.4 | async-start | bytes 8388608 | tf_op jit(solution)/shard_map/all_to_all | solution.py:34
  162.8 0.0 all-gather.2.cloned.1.call-done
  162.8 0.0 copy-start.7
  162.8 3.7 %fusion.4 = (bf16[1024,896]{1,0:T(8,128)(2,1)S(1)}, bf16[1024,896]{1,0:T(8,128)(2,1)S(1)}) fusion(bf16[4,256,896]{2,1,0:T(8,128)(2,1)S(1)} %all_to_all.43, bf16[1024,1792]{1,0:T(8,128)(2,1)} %all-gather.2.cloned.1.call-done), kind=kLoop, calls=%fused_computation.11 | loop fusion | flops 14680064 | bytes 9175040 | tf_op jit(solution)/shard_map/convert_element_type | solution.py:16
  166.5 0.0 copy-start.2
  166.5 0.0 copy-start
  166.6 0.0 copy-done.7
  166.6 0.0 copy-start.8
  166.6 4.5 %fusion.12 = f32[1024,2048]{1,0:T(8,128)S(1)} fusion(bf16[1024,896]{1,0:T(8,128)(2,1)S(1)} %get-tuple-element.9, bf16[2048,896]{1,0:T(8,128)(2,1)S(1)} %copy-done.7), kind=kOutput, calls=%fused_computation.23 | convolution fusion | flops 3758096384 | bytes 13893632 | tf_op jit(solution)/shard_map/dot_general | solution.py:21
  171.1 0.0 copy-done.2
  171.1 0.0 copy-done
  171.1 0.0 copy-done.8
  171.1 6.2 %add_convert_fusion = bf16[1024,2048]{1,0:T(8,128)(2,1)} fusion(f32[1024,2048]{1,0:T(8,128)S(1)} %fusion.12, bf16[1024,896]{1,0:T(8,128)(2,1)S(1)} %get-tuple-element.8, bf16[2048,896]{1,0:T(8,128)(2,1)S(1)} %copy-done.8), kind=kOutput, calls=%fused_computation | convolution fusion | flops 3762290688 | bytes 18087936 | tf_op jit(solution)/shard_map/dot_general | solution.py:21
  177.3 40.7 %all-to-all-done.4 = bf16[32,32,2048]{2,1,0:T(8,128)(2,1)} async-done(((bf16[32,32,2048]{2,1,0:T(8,128)(2,1)}), bf16[32,32,2048]{2,1,0:T(8,128)(2,1)}, u32[]{:S(2)}, u32[]{:S(2)}) %all-to-all-start.4) | async-done | bytes 4194336 | tf_op jit(solution)/shard_map/all_to_all | solution.py:34
  218.0 5.8 %all-to-all-start.3 = ((bf16[32,32,2048]{2,1,0:T(8,128)(2,1)}), bf16[32,32,2048]{2,1,0:T(8,128)(2,1)}, u32[]{:S(2)}, u32[]{:S(2)}) async-start(bf16[32,32,2048]{2,1,0:T(8,128)(2,1)} %bitcast.23), calls=%async_computation.3 | async-start | bytes 8388608 | tf_op jit(solution)/shard_map/all_to_all | solution.py:38
  223.8 0.0 copy-start.3
  223.8 9.5 %convolution_convert_fusion = bf16[896,2048]{1,0:T(8,128)(2,1)} fusion(bf16[1024,2048]{1,0:T(8,128)(2,1)} %bitcast, bf16[1024,1792]{1,0:T(8,128)(2,1)} %all-gather.2.cloned.1.call-done), kind=kOutput, calls=%fused_computation.18 | convolution fusion | flops 3767271424 | bytes 11534336 | tf_op jit(solution)/shard_map/dot_general | solution.py:27
  233.3 0.0 copy-done.3
  233.3 8.1 %convert_bitcast_fusion.1 = bf16[2048,896]{0,1:T(8,128)(2,1)} fusion(bf16[1024,896]{1,0:T(8,128)(2,1)S(1)} %copy-done.3, bf16[1024,2048]{1,0:T(8,128)(2,1)} %bitcast.5), kind=kOutput, calls=%fused_computation.17 | convolution fusion | flops 3759931392 | bytes 9699328 | tf_op jit(solution)/shard_map/dot_general | solution.py:27
  241.4 0.0 copy-start.1
  241.4 6.2 %copy.11 = bf16[2048,896]{1,0:T(8,128)(2,1)} copy(bf16[2048,896]{0,1:T(8,128)(2,1)} %convert_bitcast_fusion.1) | data formatting | bytes 7340032
  247.5 0.0 copy-done.1
  247.6 8.0 %convert_bitcast_fusion = bf16[2048,896]{0,1:T(8,128)(2,1)} fusion(bf16[1024,896]{1,0:T(8,128)(2,1)S(1)} %copy-done.1, bf16[1024,2048]{1,0:T(8,128)(2,1)} %bitcast.5), kind=kOutput, calls=%fused_computation.16 | convolution fusion | flops 3759931392 | bytes 9699328 | tf_op jit(solution)/shard_map/dot_general | solution.py:27
  255.6 6.0 %copy.12 = bf16[2048,896]{1,0:T(8,128)(2,1)} copy(bf16[2048,896]{0,1:T(8,128)(2,1)} %convert_bitcast_fusion) | data formatting | bytes 7340032
  261.6 18.5 %all-to-all-done.3 = bf16[32,32,2048]{2,1,0:T(8,128)(2,1)} async-done(((bf16[32,32,2048]{2,1,0:T(8,128)(2,1)}), bf16[32,32,2048]{2,1,0:T(8,128)(2,1)}, u32[]{:S(2)}, u32[]{:S(2)}) %all-to-all-start.3) | async-done | bytes 4194336 | tf_op jit(solution)/shard_map/all_to_all | solution.py:38
  280.1 3.7 %reduce_sum.25 = bf16[32,2048]{1,0:T(8,128)(2,1)} reduce(bf16[32,32,2048]{2,1,0:T(8,128)(2,1)} %all-to-all-done.3, bf16[]{:T(256)} %constant.4.clone.1), dimensions={0}, to_apply=%region_1.0 | reduce | flops 2031616 | bytes 4325378 | tf_op jit(solution)/shard_map/reduce_sum | solution.py:40
Async XLA Ops:
  10.6 9.8 %copy-start.4 = (bf16[256,896]{1,0:T(8,128)(2,1)S(1)}, bf16[256,896]{1,0:T(8,128)(2,1)}, u32[]{:S(2)}) copy-start(bf16[256,896]{1,0:T(8,128)(2,1)} %param.10) | copy-start | bytes 1376260
  10.6 9.8 %copy-start.5 = (bf16[256,896]{1,0:T(8,128)(2,1)S(1)}, bf16[256,896]{1,0:T(8,128)(2,1)}, u32[]{:S(2)}) copy-start(bf16[256,896]{1,0:T(8,128)(2,1)} %param.9) | copy-start | bytes 1376260
  10.6 77.2 %all-to-all-start = ((bf16[32,32,2048]{2,1,0:T(8,128)(2,1)}), bf16[32,32,2048]{2,1,0:T(8,128)(2,1)}, u32[]{:S(2)}, u32[]{:S(2)}) async-start(bf16[32,32,2048]{2,1,0:T(8,128)(2,1)} %tile.6), calls=%async_computation | async-start | bytes 8388608 | tf_op jit(solution)/shard_map/all_to_all | solution.py:34
  20.3 142.5 %all-gather.2.cloned.1.call-start = ((), (), s32[]{:S(2)}) async-start(), calls=%async_computation.5 | async-start | bytes 4587520 | tf_op jit(solution)/shard_map/all_gather | solution.py:52
  123.2 27.5 %copy-start.6 = (bf16[32,2048]{1,0:T(8,128)(2,1)S(1)}, bf16[32,2048]{1,0:T(8,128)(2,1)}, u32[]{:S(2)}) copy-start(bf16[32,2048]{1,0:T(8,128)(2,1)} %param.7) | copy-start | bytes 393220
  153.1 64.9 %all-to-all-start.4 = ((bf16[32,32,2048]{2,1,0:T(8,128)(2,1)}), bf16[32,32,2048]{2,1,0:T(8,128)(2,1)}, u32[]{:S(2)}, u32[]{:S(2)}) async-start(bf16[32,32,2048]{2,1,0:T(8,128)(2,1)} %tile.8), calls=%async_computation.4 | async-start | bytes 8388608 | tf_op jit(solution)/shard_map/all_to_all | solution.py:34
  162.8 3.7 %copy-start.7 = (bf16[2048,896]{1,0:T(8,128)(2,1)S(1)}, bf16[2048,896]{1,0:T(8,128)(2,1)}, u32[]{:S(2)}) copy-start(bf16[2048,896]{1,0:T(8,128)(2,1)} %param.11) | copy-start | bytes 11010052
  166.5 4.6 %copy-start.2 = (bf16[1024,896]{1,0:T(8,128)(2,1)}, bf16[1024,896]{1,0:T(8,128)(2,1)S(1)}, u32[]{:S(2)}) copy-start(bf16[1024,896]{1,0:T(8,128)(2,1)S(1)} %get-tuple-element.9) | copy-start | bytes 5505028
  166.5 4.6 %copy-start = (bf16[1024,896]{1,0:T(8,128)(2,1)}, bf16[1024,896]{1,0:T(8,128)(2,1)S(1)}, u32[]{:S(2)}) copy-start(bf16[1024,896]{1,0:T(8,128)(2,1)S(1)} %get-tuple-element.8) | copy-start | bytes 5505028
  166.6 4.6 %copy-start.8 = (bf16[2048,896]{1,0:T(8,128)(2,1)S(1)}, bf16[2048,896]{1,0:T(8,128)(2,1)}, u32[]{:S(2)}) copy-start(bf16[2048,896]{1,0:T(8,128)(2,1)} %param.12) | copy-start | bytes 11010052
  218.0 62.1 %all-to-all-start.3 = ((bf16[32,32,2048]{2,1,0:T(8,128)(2,1)}), bf16[32,32,2048]{2,1,0:T(8,128)(2,1)}, u32[]{:S(2)}, u32[]{:S(2)}) async-start(bf16[32,32,2048]{2,1,0:T(8,128)(2,1)} %bitcast.23), calls=%async_computation.3 | async-start | bytes 8388608 | tf_op jit(solution)/shard_map/all_to_all | solution.py:38
  223.8 9.5 %copy-start.3 = (bf16[1024,896]{1,0:T(8,128)(2,1)S(1)}, bf16[1024,896]{1,0:T(8,128)(2,1)}, u32[]{:S(2)}) copy-start(bf16[1024,896]{1,0:T(8,128)(2,1)} %copy-done.2) | copy-start | bytes 5505028
  241.4 6.2 %copy-start.1 = (bf16[1024,896]{1,0:T(8,128)(2,1)S(1)}, bf16[1024,896]{1,0:T(8,128)(2,1)}, u32[]{:S(2)}) copy-start(bf16[1024,896]{1,0:T(8,128)(2,1)} %copy-done) | copy-start | bytes 5505028
Sparse Core Ops, SparseCore 0:
  23.4 55.1 all-gather.1
